TPU v7x, 512 devices: a whole 4x4x16 slice. The times are simulated.
512 devices in a mesh: tm: 32 (over z, x_hi), fsdp: 16 (over y, x_lo, core).
Axes of the slice: x: 4 (x_hi: 2, x_lo: 2; x = x_hi * 2 + x_lo), y: 4, z: 16, core: 2. Of those that a mesh axis runs over, the one named last changes fastest.
Arguments:
- latents: bfloat16 [32768, 3072], P(('tm', 'fsdp')), may hold values from -6 to 6
- projected: bfloat16 [32768, 3, 2048], P(('tm', 'fsdp')), may hold values from -20 to 20
- out_weight: bfloat16 [2048, 3072], P(None, 'fsdp'), may hold values from -0.5 to 0.5
- gate_table: float32 [40, 3072], replicated, may hold values from 0.25 to 2
- timesteps: int32 [128], P('tm'), may hold values from 0 to 39
Outputs:
- updated: bfloat16 [32768, 3072], P(('tm', 'fsdp'))
All inputs are finite; a program needn't handle non-finite values.
Results may differ from a plain program's by a relative error of at most 0.0085.
Values may be sent and summed in bfloat16 or wider, within the bound.
No kernel may reach another device: no remote copies, remote signals or barrier semaphores. Data moves between devices by JAX's collectives and lax.ppermute only.
A program may use at most 64 MiB of HBM per device.

v0:
```python
import jax
import jax.numpy as jnp
from jax import lax
from jax.sharding import PartitionSpec as P

FRAME_TOK = 256


def passed_along(value, axis, steps):
    count = lax.axis_size(axis)
    initial, last = (max(0, -steps), min(count, count - steps))
    return lax.ppermute(value, axis, [(source, source + steps) for source in range(initial, last)])


def attend(queries, extended, first_frame, frame_count):
    pair_rows = 2 * FRAME_TOK
    key_count = 5 * FRAME_TOK
    score_scale = queries.shape[1] ** (-0.5)
    row_frame = jnp.arange(pair_rows, dtype=jnp.int32) // FRAME_TOK
    col_frame = jnp.arange(key_count, dtype=jnp.int32) // FRAME_TOK

    def frame_pair(pair_index):
        offset = pair_index * pair_rows
        query_block = lax.dynamic_slice_in_dim(queries, offset, pair_rows, 0)
        window = lax.dynamic_slice_in_dim(extended, offset, key_count, 0)
        key_block = window[:, 0]
        value_block = window[:, 1]
        scores = (
            lax.dot_general(
                query_block, key_block, (((1,), (1,)), ((), ())), preferred_element_type=jnp.float32
            )
            * score_scale
        )
        distance = col_frame[None, :] - row_frame[:, None]
        existing = first_frame + 2 * pair_index + col_frame - 3 >= 0
        allowed = (distance >= 0) & (distance <= 3) & existing[None, :]
        scores = jnp.where(allowed, scores, -1e30)
        row_max = jnp.max(scores, axis=-1, keepdims=True)
        weights = jnp.exp(scores - row_max)
        row_sum = jnp.sum(weights, axis=-1, keepdims=True)
        probability = (weights / row_sum).astype(jnp.bfloat16)
        return jnp.dot(probability, value_block, preferred_element_type=jnp.float32).astype(
            jnp.bfloat16
        )

    blocks = lax.map(frame_pair, jnp.arange(frame_count // 2, dtype=jnp.int32))
    return blocks.reshape(frame_count * FRAME_TOK, queries.shape[1])


def body(latents, projected, out_weight, gate_table, timesteps):
    row_count = latents.shape[0]
    frame_count = timesteps.shape[0]
    group_tokens = frame_count * FRAME_TOK
    head_view = lax.all_to_all(projected, "fsdp", split_axis=2, concat_axis=0, tiled=True)
    queries = head_view[:, 0]
    key_values = head_view[:, 1:3]
    trailing = passed_along(key_values[group_tokens - 3 * FRAME_TOK :], "tm", 1)
    extended = jnp.concatenate([trailing, key_values], axis=0)
    first_frame = lax.axis_index("tm") * frame_count
    attended = attend(queries, extended, first_frame, frame_count)
    gathered_heads = lax.all_to_all(attended, "fsdp", split_axis=0, concat_axis=1, tiled=True)
    update = jnp.dot(
        gathered_heads,
        lax.all_gather(out_weight, "fsdp", axis=1, tiled=True),
        preferred_element_type=jnp.float32,
    )
    step_count = gate_table.shape[0]
    step_onehot = (timesteps[:, None] == jnp.arange(step_count, dtype=jnp.int32)[None, :]).astype(
        jnp.float32
    )
    frame_gates = jnp.dot(step_onehot, gate_table, precision=lax.Precision.HIGHEST)
    row_frame = (
        lax.axis_index("fsdp") * row_count + jnp.arange(row_count, dtype=jnp.int32)
    ) // FRAME_TOK
    row_onehot = (row_frame[:, None] == jnp.arange(frame_count, dtype=jnp.int32)[None, :]).astype(
        jnp.float32
    )
    row_gates = jnp.dot(row_onehot, frame_gates, precision=lax.Precision.HIGHEST)
    return (latents.astype(jnp.float32) + row_gates * update).astype(jnp.bfloat16)


def solution(mesh):
    in_specs = (
        P(("tm", "fsdp"), None),
        P(("tm", "fsdp"), None, None),
        P(None, "fsdp"),
        P(),
        P("tm"),
    )
    out_specs = P(("tm", "fsdp"), None)
    return jax.shard_map(body, mesh=mesh, in_specs=in_specs, out_specs=out_specs, check_vma=False)
```

profile of v0, /device:TPU:1, one launch (start us, length us, event | category | flops | bytes accessed | tf_op | source)
XLA Modules:
  0.0 122.3 jit_solution(10871948725285879211)
XLA Ops:
  6.5 0.0 copy-start
  6.5 0.0 all-gather.2.cloned.1.call-start
  6.5 0.7 all-gather.2.cloned.1.call-update
  7.3 2.9 %copy.9 = bf16[64,3,2048]{0,1,2:T(4,128)(2,1)S(1)} copy(bf16[64,3,2048]{2,0,1:T(8,128)(2,1)} %param.8) | data formatting | bytes 1572864 | tf_op args[1]
  10.1 2.5 %reshape.39 = bf16[16,2,12288]{2,1,0:T(2,128)(2,1)} reshape(bf16[2048,3,64]{2,1,0:T(4,128)(2,1)S(1)} %bitcast.45) | data formatting | bytes 1572864
  12.6 10.3 %all-to-all-start = ((bf16[16,2,12288]{2,1,0:T(2,128)(2,1)}), bf16[16,2,12288]{2,1,0:T(2,128)(2,1)S(1)}, u32[]{:S(2)}, u32[]{:S(2)}) async-start(bf16[16,2,12288]{2,1,0:T(2,128)(2,1)} %reshape.39), calls=%async_computation | async-start | bytes 1572864 | tf_op jit(solution)/shard_map/all_to_all | solution.py:54
  22.9 0.0 copy-start.3
  22.9 13.0 %all-to-all-done = bf16[16,2,12288]{2,1,0:T(2,128)(2,1)S(1)} async-done(((bf16[16,2,12288]{2,1,0:T(2,128)(2,1)}), bf16[16,2,12288]{2,1,0:T(2,128)(2,1)S(1)}, u32[]{:S(2)}, u32[]{:S(2)}) %all-to-all-start) | async-done | bytes 786464 | tf_op jit(solution)/shard_map/all_to_all | solution.py:54
  36.0 1.3 %reshape.40 = bf16[2048,3,64]{2,1,0:T(4,128)(2,1)S(1)} reshape(bf16[16,2,12288]{2,1,0:T(2,128)(2,1)S(1)} %all-to-all-done) | data formatting | bytes 1572864
  37.2 1.2 copy.10
  38.5 1.3 %collective-permute-start = (bf16[768,2,128]{2,0,1:T(8,128)(2,1)S(1)}, bf16[768,2,128]{2,0,1:T(8,128)(2,1)S(1)}, u32[]{:S(2)}, u32[]{:S(2)}) collective-permute-start(bf16[768,2,128]{2,0,1:T(8,128)(2,1)S(1)} %slice.30), channel_id=1, source_target_pairs={{0,16},{16,32},{32,48},{48,64},{64,80},{80,96},{96,112},{112,128},... | collective-permute-start | bytes 1179656 | tf_op jit(solution)/shard_map/ppermute | solution.py:12
  39.8 0.0 copy-done
  39.8 0.0 copy-done.3
  39.8 0.3 fusion.27
  40.1 0.7 slice_bitcast_fusion
  40.9 15.6 %collective-permute-done = bf16[768,2,128]{2,0,1:T(8,128)(2,1)S(1)} collective-permute-done((bf16[768,2,128]{2,0,1:T(8,128)(2,1)S(1)}, bf16[768,2,128]{2,0,1:T(8,128)(2,1)S(1)}, u32[]{:S(2)}, u32[]{:S(2)}) %collective-permute-start) | collective-permute-done | bytes 393248 | tf_op jit(solution)/shard_map/ppermute | solution.py:12
  56.5 1.1 pad_maximum_fusion
  57.5 0.5 iota.27
  58.1 0.0 copy-start.1
  58.1 16.9 %while.14 = (s32[]{:T(128)}, bf16[2,512,128]{2,1,0:T(8,128)(2,1)}, s32[2]{0:T(128)}, s32[]{:T(128)}, bf16[1024,128]{1,0:T(8,128)(2,1)}, /*index=5*/bf16[1792,2,1...) while((s32[]{:T(128)}, bf16[2,512,128]{2,1,0:T(8,128)(2,1)}, ...), condition=%wide.region_3.4_spmd.clone.clone, body=%wide.region_0.3_spmd.clone.clone.sunk | while | flops 344156928 | bytes 8817956 | solution.py:46
  58.1 1.2 dynamic_slice.32
  60.4 2.1 %fusion.37 = (f32[512]{0:T(512)S(1)}, f32[512,1280]{1,0:T(8,128)S(1)}) fusion(bf16[1792,2,128]{2,0,1:T(8,128)(2,1)} %get-tuple-element.231, s32[]{:T(128)S(6)} %select_n.71, bf16[1024,128]{1,0:T(8,128)(2,1)} %get-tuple-element.230, s32[]{:T(128)S(6)} %select_n.72, pred[1280]{0:T(1024)(128)(4,1)S(1)} %add_compare_fusion.2, ...), kind=kOutput, calls=%fused_computation.52.clone.1 | convolution fusion | flops 173014528 | bytes 3090696 | tf_op jit(solution)/shard_map/while/body/eval_jaxpr/dot_general | solution.py:29
  62.6 0.0 copy-start.2
  62.6 0.6 copy-done.2
  63.2 1.1 fusion.38
  64.3 2.3 %fusion.39 = bf16[2,512,128]{2,1,0:T(8,128)(2,1)} fusion(bf16[2,512,128]{2,1,0:T(8,128)(2,1)} %get-tuple-element.214, s32[]{:T(128)} %get-tuple-element.213, f32[512,1280]{1,0:T(8,128)S(1)} %get-tuple-element.198, f32[512]{0:T(512)} %fusion.38, f32[512]{0:T(512)} %copy-done.2, bf16[1792,2,128]{2,0,1:T(8,128)(2,1)} %get-tuple-element.231, ...), kind=kOutput, calls=%fused_computation.14.clone.1 | convolution fusion | flops 169803776 | bytes 3084808 | tf_op jit(solution)/shard_map/while/body/eval_jaxpr/dot_general | solution.py:42
  66.5 1.2 dynamic_slice.32
  68.8 2.1 %fusion.37 = (f32[512]{0:T(512)S(1)}, f32[512,1280]{1,0:T(8,128)S(1)}) fusion(bf16[1792,2,128]{2,0,1:T(8,128)(2,1)} %get-tuple-element.231, s32[]{:T(128)S(6)} %select_n.71, bf16[1024,128]{1,0:T(8,128)(2,1)} %get-tuple-element.230, s32[]{:T(128)S(6)} %select_n.72, pred[1280]{0:T(1024)(128)(4,1)S(1)} %add_compare_fusion.2, ...), kind=kOutput, calls=%fused_computation.52.clone.1 | convolution fusion | flops 173014528 | bytes 3090696 | tf_op jit(solution)/shard_map/while/body/eval_jaxpr/dot_general | solution.py:29
  71.0 0.0 copy-start.2
  71.0 0.6 copy-done.2
  71.6 1.1 fusion.38
  72.7 2.3 %fusion.39 = bf16[2,512,128]{2,1,0:T(8,128)(2,1)} fusion(bf16[2,512,128]{2,1,0:T(8,128)(2,1)} %get-tuple-element.214, s32[]{:T(128)} %get-tuple-element.213, f32[512,1280]{1,0:T(8,128)S(1)} %get-tuple-element.198, f32[512]{0:T(512)} %fusion.38, f32[512]{0:T(512)} %copy-done.2, bf16[1792,2,128]{2,0,1:T(8,128)(2,1)} %get-tuple-element.231, ...), kind=kOutput, calls=%fused_computation.14.clone.1 | convolution fusion | flops 169803776 | bytes 3084808 | tf_op jit(solution)/shard_map/while/body/eval_jaxpr/dot_general | solution.py:42
  74.9 5.4 %all-to-all-start.1 = ((bf16[16,64,128]{2,1,0:T(8,128)(2,1)}), bf16[16,64,128]{2,1,0:T(8,128)(2,1)S(1)}, u32[]{:S(2)}, u32[]{:S(2)}) async-start(bf16[16,64,128]{2,1,0:T(8,128)(2,1)} %bitcast.49), calls=%async_computation.1 | async-start | bytes 524288 | tf_op jit(solution)/shard_map/all_to_all | solution.py:61
  80.4 0.5 fusion.25
  80.9 9.6 %all-to-all-done.1 = bf16[16,64,128]{2,1,0:T(8,128)(2,1)S(1)} async-done(((bf16[16,64,128]{2,1,0:T(8,128)(2,1)}), bf16[16,64,128]{2,1,0:T(8,128)(2,1)S(1)}, u32[]{:S(2)}, u32[]{:S(2)}) %all-to-all-start.1) | async-done | bytes 262176 | tf_op jit(solution)/shard_map/all_to_all | solution.py:61
  90.5 15.7 %all-gather.2.cloned.1.call-done = bf16[2048,3072]{0,1:T(8,128)(2,1)} async-done(((bf16[2048,192]{0,1:T(8,128)(2,1)}), bf16[2048,3072]{0,1:T(8,128)(2,1)}) %all-gather.2.cloned.1.call-update) | async-done | bytes 12582928 | tf_op jit(solution)/shard_map/all_gather | solution.py:64
  106.2 0.0 copy-done.1
  106.2 9.2 %fusion.22 = bf16[64,3072]{1,0:T(8,128)(2,1)} fusion(f32[64,3072]{1,0:T(8,128)S(1)} %fusion.25, bf16[2048,3072]{0,1:T(8,128)(2,1)} %all-gather.2.cloned.1.call-done, bf16[64,3072]{1,0:T(8,128)(2,1)S(1)} %copy-done.1, bf16[16,64,128]{2,1,0:T(8,128)(2,1)S(1)} %all-to-all-done.1), kind=kOutput, calls=%fused_computation.37 | convolution fusion | flops 806092800 | bytes 14417920 | tf_op jit(solution)/shard_map/dot_general | solution.py:62
  (10 shorter events, 0.1 us)
Async XLA Ops:
  6.5 33.3 %copy-start = (f32[40,3072]{1,0:T(8,128)S(1)}, f32[40,3072]{1,0:T(8,128)}, u32[]{:S(2)}) copy-start(f32[40,3072]{1,0:T(8,128)} %param.10) | copy-start | bytes 1474564
  6.5 99.7 %all-gather.2.cloned.1.call-start = ((), (), s32[]{:S(2)}) async-start(), calls=%async_computation.2 | async-start | bytes 13369344 | tf_op jit(solution)/shard_map/all_gather | solution.py:64
  12.6 23.3 %all-to-all-start = ((bf16[16,2,12288]{2,1,0:T(2,128)(2,1)}), bf16[16,2,12288]{2,1,0:T(2,128)(2,1)S(1)}, u32[]{:S(2)}, u32[]{:S(2)}) async-start(bf16[16,2,12288]{2,1,0:T(2,128)(2,1)} %reshape.39), calls=%async_computation | async-start | bytes 1572864 | tf_op jit(solution)/shard_map/all_to_all | solution.py:54
  22.9 16.9 %copy-start.3 = (s32[4]{0:T(128)S(1)}, s32[4]{0:T(128)}, u32[]{:S(2)}) copy-start(s32[4]{0:T(128)} %param.11) | copy-start | bytes 52
  38.5 18.0 %collective-permute-start = (bf16[768,2,128]{2,0,1:T(8,128)(2,1)S(1)}, bf16[768,2,128]{2,0,1:T(8,128)(2,1)S(1)}, u32[]{:S(2)}, u32[]{:S(2)}) collective-permute-start(bf16[768,2,128]{2,0,1:T(8,128)(2,1)S(1)} %slice.30), channel_id=1, source_target_pairs={{0,16},{16,32},{32,48},{48,64},{64,80},{80,96},{96,112},{112,128},... | collective-permute-start | bytes 1179656 | tf_op jit(solution)/shard_map/ppermute | solution.py:12
  58.1 48.2 %copy-start.1 = (bf16[64,3072]{1,0:T(8,128)(2,1)S(1)}, bf16[64,3072]{1,0:T(8,128)(2,1)}, u32[]{:S(2)}) copy-start(bf16[64,3072]{1,0:T(8,128)(2,1)} %param.7) | copy-start | bytes 1179652
  62.6 0.6 copy-start.2
  71.0 0.6 copy-start.2
  74.9 15.6 %all-to-all-start.1 = ((bf16[16,64,128]{2,1,0:T(8,128)(2,1)}), bf16[16,64,128]{2,1,0:T(8,128)(2,1)S(1)}, u32[]{:S(2)}, u32[]{:S(2)}) async-start(bf16[16,64,128]{2,1,0:T(8,128)(2,1)} %bitcast.49), calls=%async_computation.1 | async-start | bytes 524288 | tf_op jit(solution)/shard_map/all_to_all | solution.py:61
Sparse Core Ops, SparseCore 0:
  9.5 96.6 all-gather.1
where the time goes:
time: 123 us; the launch traced here: 122 us
  waiting for transfers between devices  54.7 us (44%)
  matrix products  18.8 us (15%)
  starting transfers between devices  17 us (14%)
  between operations  13.5 us (11%)
  local copies, waits for them, and re-layouts  12.7 us (10%)
  other arithmetic  3.28 us (3%)
  loops' own time  2.28 us (2%)
    all_gather x1, waiting for transfers between devices, body(): lax.all_gather(out_weight, 'fsdp', axis=1, tiled=True)  15.7 us
    ppermute x1, waiting for transfers between devices, passed_along(): lax.ppermute(value, axis, [(source, source + steps) for source in range(i...  15.6 us
    all_to_all x1, waiting for transfers between devices, body(): lax.all_to_all(projected, 'fsdp', split_axis=2, concat_axis=0, tiled=True)  13 us
    all_to_all x1, starting transfers between devices, body(): lax.all_to_all(projected, 'fsdp', split_axis=2, concat_axis=0, tiled=True)  10.3 us
    all_to_all x1, waiting for transfers between devices, body(): lax.all_to_all(attended, 'fsdp', split_axis=0, concat_axis=1, tiled=True)  9.62 us
    dot_general x1, matrix products, body(): jnp.dot(gathered_heads, lax.all_gather(out_weight, 'fsdp', axis=1, tiled=...  9.25 us
    unnamed x9, local copies, waits for them, and re-layouts  6.63 us
    all_to_all x1, starting transfers between devices, body(): lax.all_to_all(attended, 'fsdp', split_axis=0, concat_axis=1, tiled=True)  5.45 us
  transfers between devices with their start and end apart: 4, of which 4 were waited for; matrix products, arithmetic and copies ran while one was open for 20% of the time, Pallas kernels for 0%

commit v1 on v0

--- a/solution.py
+++ b/solution.py
@@ -61,7 +61,9 @@
     gathered_heads = lax.all_to_all(attended, "fsdp", split_axis=0, concat_axis=1, tiled=True)
     update = jnp.dot(
         gathered_heads,
-        lax.all_gather(out_weight, "fsdp", axis=1, tiled=True),
+        jnp.concatenate(
+            lax.all_to_all(jnp.stack([out_weight] * lax.axis_size("fsdp")), "fsdp", 0, 0), axis=1
+        ),
         preferred_element_type=jnp.float32,
     )
     step_count = gate_table.shape[0]

time: 123 us -> 230 us (1.87); the launches traced: 122 us -> 227 us
  waiting for transfers between devices: 54.7 us -> 146 us
  blocking collectives: 0 us -> 34.6 us
  between operations: 13.5 us -> 0.11 us
  starting transfers between devices: 17 us -> 7.54 us
  local copies, waits for them, and re-layouts: 12.7 us -> 15.2 us
    all_to_all x2 -> x1, waiting for transfers between devices: 22.7 us -> 139 us  [body(): lax.all_to_all(jnp.stack([out_weight] * lax.axis_size('fsdp')), 'fsdp', 0...]
    all_to_all x0 -> x2, blocking collectives: none -> 34.6 us  [the longest x1 22.1 us: body(): lax.all_to_all(projected, 'fsdp', split_axis=2, concat_axis=0, tiled=True)]
    all_gather x1 -> x0, waiting for transfers between devices: 15.7 us -> none  [body(): lax.all_gather(out_weight, 'fsdp', axis=1, tiled=True)]
    all_to_all x2 -> x1, starting transfers between devices: 15.7 us -> 5.81 us  [body(): lax.all_to_all(jnp.stack([out_weight] * lax.axis_size('fsdp')), 'fsdp', 0...]
    ppermute x1, waiting for transfers between devices: 15.6 us -> 7.3 us  [passed_along(): lax.ppermute(value, axis, [(source, source + steps) for source in range(i...]
    another operation x0 -> x1, local copies, waits for them, and re-layouts: none -> 7.22 us  [body(): jnp.stack([out_weight] * lax.axis_size('fsdp'))]
  transfers between devices with their start and end apart: 4 -> 2, of which waited for: 4 -> 2; matrix products, arithmetic and copies ran while one was open for 20% -> 0% of each run, Pallas kernels for 0% -> 0%
where the time goes in v1:
time: 230 us; the launch traced here: 227 us
  waiting for transfers between devices  146 us (63%)
  blocking collectives  34.6 us (15%)
  matrix products  18.7 us (8%)
  local copies, waits for them, and re-layouts  15.2 us (7%)
  starting transfers between devices  7.54 us (3%)
    all_to_all x1, waiting for transfers between devices, body(): lax.all_to_all(jnp.stack([out_weight] * lax.axis_size('fsdp')), 'fsdp', 0...  139 us
    all_to_all x1, blocking collectives, body(): lax.all_to_all(projected, 'fsdp', split_axis=2, concat_axis=0, tiled=True)  22.1 us
    all_to_all x1, blocking collectives, body(): lax.all_to_all(attended, 'fsdp', split_axis=0, concat_axis=1, tiled=True)  12.4 us
    dot_general x1, matrix products, body(): jnp.dot(gathered_heads, jnp.concatenate(lax.all_to_all(jnp.stack([out_wei...  9.25 us
    ppermute x1, waiting for transfers between devices, passed_along(): lax.ppermute(value, axis, [(source, source + steps) for source in range(i...  7.3 us
    another operation x1, local copies, waits for them, and re-layouts, body(): jnp.stack([out_weight] * lax.axis_size('fsdp'))  7.22 us
    all_to_all x1, starting transfers between devices, body(): lax.all_to_all(jnp.stack([out_weight] * lax.axis_size('fsdp')), 'fsdp', 0...  5.81 us
    unnamed x9, local copies, waits for them, and re-layouts  5.65 us
  transfers between devices with their start and end apart: 2, of which 2 were waited for; matrix products, arithmetic and copies ran while one was open for 0% of the time, Pallas kernels for 0%

profile of v1, /device:TPU:1, one launch (start us, length us, event | category | flops | bytes accessed | tf_op | source)
XLA Modules:
  0.0 226.6 jit_solution(4438011511154641566)
XLA Ops:
  0.0 0.0 copy-start
  0.0 2.9 %copy.10 = bf16[64,3,2048]{0,1,2:T(4,128)(2,1)S(1)} copy(bf16[64,3,2048]{2,0,1:T(8,128)(2,1)} %param.8) | data formatting | bytes 1572864 | tf_op args[1]
  2.9 1.5 reshape.49
  4.4 22.1 %all_to_all.42 = bf16[16,2,12288]{2,1,0:T(2,128)(2,1)S(1)} all-to-all(bf16[16,2,12288]{2,1,0:T(2,128)(2,1)S(1)} %reshape.49), channel_id=1, replica_groups=mesh['tm'=32,'fsdp'=16] {'fsdp'}, dimensions={0} | all-to-all | bytes 1572864 | tf_op jit(solution)/shard_map/all_to_all | solution.py:54
  26.5 1.3 reshape.50
  27.8 1.2 copy.11
  29.0 1.7 collective-permute-start
  30.9 7.3 %collective-permute-done = bf16[768,2,128]{2,0,1:T(8,128)(2,1)S(1)} collective-permute-done((bf16[768,2,128]{2,0,1:T(8,128)(2,1)S(1)}, bf16[768,2,128]{2,0,1:T(8,128)(2,1)S(1)}, u32[]{:S(2)}, u32[]{:S(2)}) %collective-permute-start) | collective-permute-done | bytes 393248 | tf_op jit(solution)/shard_map/ppermute | solution.py:12
  38.2 1.0 pad_maximum_fusion
  39.1 13.1 %while.14 = (s32[]{:T(128)}, bf16[2,512,128]{2,1,0:T(8,128)(2,1)}, s32[2]{0:T(128)S(1)}, s32[]{:T(128)}, bf16[1024,128]{1,0:T(8,128)(2,1)S(1)}, /*index=5*/bf16[...) while((s32[]{:T(128)}, bf16[2,512,128]{2,1,0:T(8,128)(2,1)}, ...), condition=%wide.region_3.4_spmd.clone.clone, body=%wide.region_0.3_spmd.clone.clone.sunk | while | flops 344156928 | bytes 8813076 | solution.py:46
  39.1 0.6 dynamic_slice.32
  40.8 2.1 fusion.37
  42.9 0.5 fusion.38
  43.4 2.2 fusion.39
  45.7 0.6 dynamic_slice.32
  47.4 2.1 fusion.37
  49.4 0.5 fusion.38
  50.0 2.2 fusion.39
  52.2 12.4 %all_to_all.43 = bf16[16,64,128]{2,1,0:T(8,128)(2,1)S(1)} all-to-all(bf16[16,64,128]{2,1,0:T(8,128)(2,1)} %bitcast.52), channel_id=1, replica_groups=mesh['tm'=32,'fsdp'=16] {'fsdp'}, dimensions={0} | all-to-all | bytes 524288 | tf_op jit(solution)/shard_map/all_to_all | solution.py:61
  64.6 7.2 %stack.2 = bf16[16,2048,192]{1,2,0:T(8,128)(2,1)} broadcast(bf16[2048,192]{0,1:T(8,128)(2,1)} %param.9), dimensions={1,2} | broadcast | bytes 13369344 | tf_op jit(solution)/shard_map/stack | solution.py:65
  71.8 0.0 copy-start.2
  71.8 0.0 copy-start.1
  71.8 5.8 %all-to-all-start.2 = ((bf16[16,2048,192]{1,2,0:T(8,128)(2,1)}), bf16[16,2048,192]{1,2,0:T(8,128)(2,1)}, u32[]{:S(2)}, u32[]{:S(2)}) async-start(bf16[16,2048,192]{1,2,0:T(8,128)(2,1)} %stack.2), calls=%async_computation.2 | async-start | bytes 25165824 | tf_op jit(solution)/shard_map/all_to_all | solution.py:65
  77.7 0.0 copy-done
  77.7 0.0 copy-done.2
  77.7 0.3 fusion.27
  78.0 0.5 fusion.25
  78.5 138.8 %all-to-all-done.2 = bf16[16,2048,192]{1,2,0:T(8,128)(2,1)} async-done(((bf16[16,2048,192]{1,2,0:T(8,128)(2,1)}), bf16[16,2048,192]{1,2,0:T(8,128)(2,1)}, u32[]{:S(2)}, u32[]{:S(2)}) %all-to-all-start.2) | async-done | bytes 12582944 | tf_op jit(solution)/shard_map/all_to_all | solution.py:65
  217.3 0.0 copy-done.1
  217.3 9.2 %fusion.22 = bf16[64,3072]{1,0:T(8,128)(2,1)} fusion(f32[64,3072]{1,0:T(8,128)S(1)} %fusion.25, bf16[2048,3072]{0,1:T(8,128)(2,1)} %bitcast.8, bf16[64,3072]{1,0:T(8,128)(2,1)S(1)} %copy-done.1, bf16[16,64,128]{2,1,0:T(8,128)(2,1)S(1)} %all_to_all.43), kind=kOutput, calls=%fused_computation.37 | convolution fusion | flops 806092800 | bytes 14417920 | tf_op jit(solution)/shard_map/dot_general | solution.py:62
  (12 shorter events, 0.1 us)
Async XLA Ops:
  0.0 77.7 %copy-start = (f32[40,3072]{1,0:T(8,128)S(1)}, f32[40,3072]{1,0:T(8,128)}, u32[]{:S(2)}) copy-start(f32[40,3072]{1,0:T(8,128)} %param.10) | copy-start | bytes 1474564
  29.0 9.1 %collective-permute-start = (bf16[768,2,128]{2,0,1:T(8,128)(2,1)S(1)}, bf16[768,2,128]{2,0,1:T(8,128)(2,1)S(1)}, u32[]{:S(2)}, u32[]{:S(2)}) collective-permute-start(bf16[768,2,128]{2,0,1:T(8,128)(2,1)S(1)} %slice.30), channel_id=1, source_target_pairs={{0,16},{16,32},{32,48},{48,64},{64,80},{80,96},{96,112},{112,128},... | collective-permute-start | bytes 1179656 | tf_op jit(solution)/shard_map/ppermute | solution.py:12
  71.8 5.8 %copy-start.2 = (s32[4]{0:T(128)S(1)}, s32[4]{0:T(128)}, u32[]{:S(2)}) copy-start(s32[4]{0:T(128)} %param.11) | copy-start | bytes 52
  71.8 145.5 %copy-start.1 = (bf16[64,3072]{1,0:T(8,128)(2,1)S(1)}, bf16[64,3072]{1,0:T(8,128)(2,1)}, u32[]{:S(2)}) copy-start(bf16[64,3072]{1,0:T(8,128)(2,1)} %param.7) | copy-start | bytes 1179652
  71.8 145.5 %all-to-all-start.2 = ((bf16[16,2048,192]{1,2,0:T(8,128)(2,1)}), bf16[16,2048,192]{1,2,0:T(8,128)(2,1)}, u32[]{:S(2)}, u32[]{:S(2)}) async-start(bf16[16,2048,192]{1,2,0:T(8,128)(2,1)} %stack.2), calls=%async_computation.2 | async-start | bytes 25165824 | tf_op jit(solution)/shard_map/all_to_all | solution.py:65
